TPU v7x, 32 devices: a whole 2x2x4 slice. The times are simulated.
32 devices in a mesh: groups: 2 (over y), paths: 4 (over z), cols: 2 (over x), depth: 2 (over core).
Axes of the slice: x: 2, y: 2, z: 4, core: 2. Of those that a mesh axis runs over, the one named last changes fastest.
Arguments:
- panels: bfloat16 [96, 64, 1024], P(('groups', 'cols', 'paths'), None, 'depth'), parts along dimension 0, may hold values from -0.0546875 to 0.0546875
- model: bfloat16 [96, 1024], P(('groups', 'cols', 'paths'), 'depth'), parts along dimension 0, may hold values from -6 to 6
- depth_weight: bfloat16 [2048, 1024], P(('groups', 'paths'), 'depth'), parts along dimension 0, may hold values from -6 to 6
- seg_len: bfloat16 [2048, 48], P(('groups', 'paths'), 'cols'), parts along dimension 0, may hold values from 0.29882812 to 3
- path_start: int32 [2048], P(('groups', 'paths')), parts along dimension 0, may hold values from 0 to 47, as said below
- path_end: int32 [2048], P(('groups', 'paths')), parts along dimension 0, may hold values from 1 to 48, as said below
- mode_index: int32 [2048, 4], P(('groups', 'paths')), parts along dimension 0, may hold values from 0 to 63, all different within a row
- observed: float32 [2048, 4], P(('groups', 'paths')), parts along dimension 0, may hold values from -6 to 6
Outputs:
- gradient: float32 [96, 1024], P(('groups', 'cols', 'paths'), 'depth'), parts along dimension 0
- misfit: float32 [2048, 4], P(('groups', 'paths')), parts along dimension 0
There are 2 independent parts, one for each index of `groups`. A program takes and returns all parts, laid end to end along the dimension named above; each array names one. Nothing has to cross between parts.
Inputs may be any that keep to these rules, and one draw needn't show every extreme that they name: `path_start`: each path starts before it ends; path 0 spans all 48 columns. `path_end`: each path ends after it starts. `mode_index`: each path names 4 different modes.
All inputs are finite; a program needn't handle non-finite values.
Results may differ from a plain program's by a relative error of at most 0.011.
Values may be sent and summed in bfloat16 or wider, within the bound.
No kernel may reach another device: no remote copies, remote signals or barrier semaphores. Data moves between devices by JAX's collectives and lax.ppermute only.
A program may use at most 64 MiB of HBM per device.

v0:
```python
import jax
import jax.numpy as jnp
from jax import lax
from jax.sharding import PartitionSpec as P


def finish(partial_value, one_hot, observed):
    combined = lax.psum(partial_value, ("cols", "depth"))
    travel = jnp.einsum("pkm,pm->pk", one_hot, combined)
    misfit = travel - observed
    resid_modes = jnp.einsum("pk,pkm->pm", misfit, one_hot)
    return (misfit, resid_modes)


def shards(panels, model, depth_weight, seg_len, path_start, path_end, mode_index, observed):
    own_cols, modes, depth_half = panels.shape
    path_rows, block_cols = seg_len.shape
    columns = lax.axis_index("cols") * block_cols + lax.iota(jnp.int32, block_cols)
    inside = (columns[None, :] >= path_start[:, None]) & (columns[None, :] < path_end[:, None])
    lengths = jnp.where(inside, seg_len, jnp.zeros_like(seg_len))
    one_hot = (mode_index[:, :, None] == lax.iota(jnp.int32, modes)[None, None, :]).astype(
        jnp.float32
    )
    kernel_piece = lax.all_gather(panels, "paths", axis=0, tiled=True)
    model_piece = lax.all_gather(model, "paths", axis=0, tiled=True)
    row_count = kernel_piece.shape[0]
    scaled = (
        kernel_piece.astype(jnp.float32) * model_piece.astype(jnp.float32)[:, None, :]
    ).astype(jnp.bfloat16)
    scaled = scaled.reshape(row_count * modes, depth_half)
    weighted = lax.dot_general(
        depth_weight, scaled, (((1,), (1,)), ((), ())), preferred_element_type=jnp.float32
    )
    weighted = weighted.reshape(path_rows, row_count, modes)
    row_weights = lengths.astype(jnp.float32)
    partial_value = jnp.einsum("pc,pcm->pm", row_weights, weighted)
    misfit, resid_modes = finish(partial_value, one_hot, observed)
    kernel_piece = lax.all_gather(panels, "paths", axis=0, tiled=True)
    row_count = kernel_piece.shape[0]
    row_weights = lengths.astype(jnp.float32)
    spread = (
        (row_weights[:, :, None] * resid_modes[:, None, :])
        .astype(jnp.bfloat16)
        .reshape(path_rows, row_count * modes)
    )
    summed = lax.dot_general(
        spread, depth_weight, (((0,), (0,)), ((), ())), preferred_element_type=jnp.float32
    )
    summed = summed.reshape(row_count, modes, depth_half)
    block_terms = jnp.sum(summed * kernel_piece.astype(jnp.float32), axis=1)
    gradient = lax.psum_scatter(block_terms, "paths", scatter_dimension=0, tiled=True)
    return (gradient, misfit)


def solution(mesh):
    return jax.shard_map(
        shards,
        mesh=mesh,
        in_specs=(
            P(("groups", "cols", "paths"), None, "depth"),
            P(("groups", "cols", "paths"), "depth"),
            P(("groups", "paths"), "depth"),
            P(("groups", "paths"), "cols"),
            P(("groups", "paths")),
            P(("groups", "paths")),
            P(("groups", "paths"), None),
            P(("groups", "paths"), None),
        ),
        out_specs=(P(("groups", "cols", "paths"), "depth"), P(("groups", "paths"), None)),
        check_vma=False,
    )
```

profile of v0, /device:TPU:0, one launch (start us, length us, event | category | flops | bytes accessed | tf_op | source)
XLA Modules:
  0.0 111.6 jit_solution(14641012471253387348)
XLA Ops:
  7.2 0.0 copy-start
  7.2 0.0 all-gather.3.cloned.1.call-start
  7.2 0.7 all-gather.3.cloned.1.call-update
  7.9 0.0 all-reduce.4.cloned.1.call-start
  8.0 15.0 %all-gather = bf16[4,6,512]{2,1,0:T(8,128)(2,1)S(1)} all-gather(bf16[1,6,512]{2,1,0:T(8,128)(2,1)} %bitcast.28), channel_id=1, replica_groups=mesh['groups'=2,'paths'=4,'cols'=2,'depth'=2] {'paths'}, dimensions={0}, use_global_device_ids=true | all-gather | bytes 30720 | tf_op jit(solution)/shard_map/all_gather | solution.py:25
  23.0 0.8 fusion.10
  23.8 25.6 %all-gather.3.cloned.1.call-done = bf16[24,64,512]{2,1,0:T(8,128)(2,1)} async-done(((bf16[6,64,512]{2,1,0:T(8,128)(2,1)}), bf16[24,64,512]{2,1,0:T(8,128)(2,1)}) %all-gather.3.cloned.1.call-update) | async-done | bytes 1572880 | tf_op jit(solution)/shard_map/all_gather | solution.py:24
  49.4 1.7 %fusion.1 = bf16[24,64,512]{2,1,0:T(8,128)(2,1)S(1)} fusion(bf16[24,64,512]{2,1,0:T(8,128)(2,1)} %all-gather.3.cloned.1.call-done, f32[24,512]{1,0:T(8,128)S(1)} %reshape.31), kind=kLoop, calls=%fused_computation.2 | loop fusion | flops 2359296 | bytes 3194880 | tf_op jit(solution)/shard_map/convert_element_type | solution.py:29
  51.2 0.0 copy-done
  51.2 0.6 fusion.11
  51.8 0.0 copy-start.3
  51.8 0.1 multiply_reduce_fusion
  51.9 0.0 copy-start.4
  52.0 0.8 copy.17
  52.7 0.0 copy-start.1
  52.7 0.0 all-reduce.4.cloned.1.call-update
  52.7 0.0 copy-done.3
  52.7 0.1 copy.12
  52.9 30.3 %all-reduce.4.cloned.1.call-done = f32[256,64]{1,0:T(8,128)} async-done(((f32[256,64]{1,0:T(8,128)}), f32[256,64]{1,0:T(8,128)}) %all-reduce.4.cloned.1.call-update) | async-done | bytes 65552 | tf_op jit(solution)/shard_map/psum | solution.py:8
  83.2 1.4 %fusion.7 = f32[256,1,4]{2,1,0:T(1,128)S(1)} fusion(f32[256,64,1]{1,2,0:T(1,128)} %bitcast.29, s32[256,4]{1,0:T(8,128)S(1)} %copy.12), kind=kOutput, calls=%fused_computation.11 | convolution fusion | flops 196608 | bytes 73728 | tf_op jit(solution)/shard_map/pkm,pm->pk/dot_general | solution.py:9
  84.6 0.1 copy.19
  84.7 0.0 copy-done.4
  84.7 0.0 copy-start.2
  84.7 0.1 copy.26
  84.8 1.4 %select_reduce_fusion = f32[256,64]{1,0:T(8,128)S(1)} fusion(f32[256,4]{1,0:T(8,128)S(1)} %copy.26, s32[256,4]{1,0:T(8,128)S(1)} %copy.12), kind=kLoop, calls=%fused_computation.9 | loop fusion | flops 180224 | bytes 73728
  86.3 0.1 copy.23
  86.4 0.0 copy-done.1
  86.4 0.0 copy-start.5
  86.4 0.6 fusion.2
  87.0 0.0 copy-done.2
  87.0 12.8 %fusion = f32[8,512]{1,0:T(8,128)S(1)} fusion(f32[24,512]{1,0:T(8,128)S(1)} %fusion.2), kind=kCustom, calls=%all-reduce-scatter | all-reduce-scatter fusion | flops 16385 | bytes 66048
  99.8 2.9 %collective-permute-start = (f32[6,512]{1,0:T(8,128)S(1)}, f32[6,512]{1,0:T(8,128)S(1)}, u32[]{:S(2)}, u32[]{:S(2)}) collective-permute-start(f32[6,512]{1,0:T(8,128)S(1)} %slice), channel_id=1, source_target_pairs={{0,4},{4,8},{8,12},{1,5},{5,9},{9,13},{2,6},{6,10},{10,14},{3,7},{... | collective-permute-start | bytes 36872
  102.7 0.0 copy-done.5
  102.7 0.6 dynamic-slice.4
  103.9 0.2 collective-permute-done
  104.1 0.1 concatenate
  104.2 0.6 constant_dynamic-slice_fusion
  (4 shorter events, 0.0 us)
Async XLA Ops:
  7.2 44.0 %copy-start = (bf16[256,512]{1,0:T(8,128)(2,1)S(1)}, bf16[256,512]{1,0:T(8,128)(2,1)}, u32[]{:S(2)}) copy-start(bf16[256,512]{1,0:T(8,128)(2,1)} %param.10) | copy-start | bytes 786436
  7.2 42.2 %all-gather.3.cloned.1.call-start = ((), (), s32[]{:S(2)}) async-start(), calls=%async_computation | async-start | bytes 1966080 | tf_op jit(solution)/shard_map/all_gather | solution.py:24
  7.9 75.2 %all-reduce.4.cloned.1.call-start = ((), (), s32[]{:S(2)}) async-start(), calls=%async_computation.1 | async-start | bytes 262144 | tf_op jit(solution)/shard_map/psum | solution.py:8
  51.8 1.0 copy-start.3
  51.9 32.7 %copy-start.4 = (f32[256,4]{0,1:T(4,128)S(1)}, f32[256,4]{0,1:T(4,128)}, u32[]{:S(2)}) copy-start(f32[256,4]{0,1:T(4,128)} %param.15) | copy-start | bytes 12292
  52.7 33.7 %copy-start.1 = (bf16[24,64,512]{2,1,0:T(8,128)(2,1)S(1)}, bf16[24,64,512]{2,1,0:T(8,128)(2,1)}, u32[]{:S(2)}) copy-start(bf16[24,64,512]{2,1,0:T(8,128)(2,1)} %all-gather.3.cloned.1.call-done) | copy-start | bytes 4718596
  84.7 2.3 %copy-start.2 = (f32[256,4]{0,1:T(4,128)}, f32[256,4]{0,1:T(4,128)S(1)}, u32[]{:S(2)}) copy-start(f32[256,4]{0,1:T(4,128)S(1)} %bitcast_subtract_fusion) | copy-start | bytes 12292
  86.4 16.3 %copy-start.5 = (u32[32]{0:T(128)S(1)}, u32[32]{0:T(128)}, u32[]{:S(2)}) copy-start(u32[32]{0:T(128)} %constant.17) | copy-start | bytes 388
  99.8 4.3 %collective-permute-start = (f32[6,512]{1,0:T(8,128)S(1)}, f32[6,512]{1,0:T(8,128)S(1)}, u32[]{:S(2)}, u32[]{:S(2)}) collective-permute-start(f32[6,512]{1,0:T(8,128)S(1)} %slice), channel_id=1, source_target_pairs={{0,4},{4,8},{8,12},{1,5},{5,9},{9,13},{2,6},{6,10},{10,14},{3,7},{... | collective-permute-start | bytes 36872
Sparse Core Ops, SparseCore 0:
  9.6 39.7 all-gather.2
  52.9 30.2 all-reduce.3
where the time goes:
time: 112 us
  waiting for transfers between devices  56.8 us (51%)
  blocking collectives  27.8 us (25%)
  between operations  14.9 us (13%)
  other arithmetic  4.14 us (4%)
  starting transfers between devices  2.94 us (3%)
  matrix products  2.64 us (2%)
  local copies, waits for them, and re-layouts  2.5 us (2%)
    psum x1, waiting for transfers between devices, finish(): combined = lax.psum(partial_value, ('cols', 'depth'))  30.3 us
    all_gather x1, waiting for transfers between devices, shards(): kernel_piece = lax.all_gather(panels, 'paths', axis=0, tiled=True)  25.6 us
    all_gather x1, blocking collectives, shards(): model_piece = lax.all_gather(model, 'paths', axis=0, tiled=True)  15 us
    unnamed x1, blocking collectives  12.8 us
    unnamed x1, starting transfers between devices  2.87 us
  transfers between devices with their start and end apart: 3, of which 3 were waited for; matrix products, arithmetic and copies ran while one was open for 1% of the time, Pallas kernels for 0%

commit v1 on v0

--- a/solution.py
+++ b/solution.py
@@ -1,11 +1,20 @@
+import functools
 import jax
 import jax.numpy as jnp
 from jax import lax
 from jax.sharding import PartitionSpec as P
 
 
+def view_files(message, lane_axis):
+    block_next = lax.all_gather(message, lane_axis)
+    return jnp.sum(block_next, axis=0)
+
+
+_carry_members_all = functools.partial(view_files, lane_axis=("cols", "depth"))
+
+
 def finish(partial_value, one_hot, observed):
-    combined = lax.psum(partial_value, ("cols", "depth"))
+    combined = _carry_members_all(partial_value)
     travel = jnp.einsum("pkm,pm->pk", one_hot, combined)
     misfit = travel - observed
     resid_modes = jnp.einsum("pk,pkm->pm", misfit, one_hot)

time: 112 us -> 84.8 us (0.76)
  waiting for transfers between devices: 56.8 us -> 25.7 us
  blocking collectives: 27.8 us -> 33.2 us
  matrix products: 2.64 us -> 1.23 us
  starting transfers between devices: 2.94 us -> 1.7 us
    psum x1 -> x0, waiting for transfers between devices: 30.3 us -> none  [finish(): combined = lax.psum(partial_value, ('cols', 'depth'))]
    all_gather x0 -> x1, blocking collectives: none -> 5.92 us  [view_files(): block_next = lax.all_gather(message, lane_axis)]
    dot_general x1 -> x0, matrix products: 1.42 us -> none  [finish(): travel = jnp.einsum('pkm,pm->pk', one_hot, combined)]
    unnamed x1, starting transfers between devices: 2.87 us -> 1.66 us
    unnamed x18 -> x17, local copies, waits for them, and re-layouts: 1.58 us -> 2.35 us
  transfers between devices with their start and end apart: 3 -> 2, of which waited for: 3 -> 2; matrix products, arithmetic and copies ran while one was open for 1% -> 3% of each run, Pallas kernels for 0% -> 0%
where the time goes in v1:
time: 84.8 us; the launch traced here: 84.5 us
  blocking collectives  33.2 us (39%)
  waiting for transfers between devices  25.7 us (30%)
  between operations  14.9 us (18%)
  other arithmetic  5.19 us (6%)
  local copies, waits for them, and re-layouts  2.64 us (3%)
  starting transfers between devices  1.7 us (2%)
  matrix products  1.23 us (1%)
    all_gather x1, waiting for transfers between devices, shards(): kernel_piece = lax.all_gather(panels, 'paths', axis=0, tiled=True)  24.8 us
    all_gather x1, blocking collectives, shards(): model_piece = lax.all_gather(model, 'paths', axis=0, tiled=True)  15 us
    unnamed x1, blocking collectives  12.3 us
    all_gather x1, blocking collectives, view_files(): block_next = lax.all_gather(message, lane_axis)  5.92 us
    unnamed x17, local copies, waits for them, and re-layouts  2.35 us
    unnamed x2, other arithmetic  2.34 us
    convert_element_type x1, other arithmetic, shards(): scaled = (kernel_piece.astype(jnp.float32) * model_piece.astype(jnp.float...  1.74 us
  transfers between devices with their start and end apart: 2, of which 2 were waited for; matrix products, arithmetic and copies ran while one was open for 3% of the time, Pallas kernels for 0%

profile of v1, /device:TPU:0, one launch (start us, length us, event | category | flops | bytes accessed | tf_op | source)
XLA Modules:
  0.0 84.5 jit_solution(5725507183063496644)
XLA Ops:
  7.2 0.0 copy-start
  7.2 0.0 all-gather.4.cloned.1.call-start
  7.2 0.7 all-gather.4.cloned.1.call-update
  7.9 15.0 %all-gather.1 = bf16[4,6,512]{2,1,0:T(8,128)(2,1)S(1)} all-gather(bf16[1,6,512]{2,1,0:T(8,128)(2,1)} %bitcast.28), channel_id=1, replica_groups=mesh['groups'=2,'paths'=4,'cols'=2,'depth'=2] {'paths'}, dimensions={0}, use_global_device_ids=true | all-gather | bytes 30720 | tf_op jit(solution)/shard_map/all_gather | solution.py:34
  23.0 0.8 copy.14
  23.8 0.8 fusion.9
  24.6 24.8 %all-gather.4.cloned.1.call-done = bf16[24,64,512]{2,1,0:T(8,128)(2,1)} async-done(((bf16[6,64,512]{2,1,0:T(8,128)(2,1)}), bf16[24,64,512]{2,1,0:T(8,128)(2,1)}) %all-gather.4.cloned.1.call-update) | async-done | bytes 1572880 | tf_op jit(solution)/shard_map/all_gather | solution.py:33
  49.4 1.7 %fusion.1 = bf16[24,64,512]{2,1,0:T(8,128)(2,1)S(1)} fusion(bf16[24,64,512]{2,1,0:T(8,128)(2,1)} %all-gather.4.cloned.1.call-done, f32[24,512]{1,0:T(8,128)S(1)} %reshape.32), kind=kLoop, calls=%fused_computation.2 | loop fusion | flops 2359296 | bytes 3194880 | tf_op jit(solution)/shard_map/convert_element_type | solution.py:38
  51.2 0.0 copy-done
  51.2 0.6 fusion.10
  51.8 0.0 copy-start.3
  51.8 0.1 multiply_reduce_fusion
  51.9 0.0 copy-start.1
  52.0 5.9 %all-gather = f32[1024,64]{0,1:T(8,128)S(1)} all-gather(f32[256,64]{0,1:T(8,128)S(1)} %multiply_reduce_fusion), channel_id=2, replica_groups=mesh['groups'=2,'paths'=4,'cols'=2,'depth'=2] {'cols','depth'}, dimensions={0}, use_global_device_ids=true | all-gather | bytes 327680 | tf_op jit(solution)/shard_map/all_gather | solution.py:9
  57.9 0.1 reshape.29
  58.0 0.2 reduce_sum.18
  58.2 0.1 copy.31
  58.3 0.9 %select_reduce_fusion.1 = f32[256,4]{1,0:T(8,128)S(1)} fusion(f32[256,64]{1,0:T(8,128)S(1)} %copy.31, s32[256,4]{1,0:T(8,128)S(1)} %copy.14), kind=kLoop, calls=%fused_computation.10 | loop fusion | flops 195584 | bytes 73728
  59.2 0.1 copy.24
  59.2 0.0 copy-done.3
  59.2 0.0 copy-start.2
  59.3 0.1 copy.33
  59.4 1.4 %select_reduce_fusion = f32[256,64]{1,0:T(8,128)S(1)} fusion(f32[256,4]{1,0:T(8,128)S(1)} %copy.33, s32[256,4]{1,0:T(8,128)S(1)} %copy.14), kind=kLoop, calls=%fused_computation.9 | loop fusion | flops 180224 | bytes 73728
  60.9 0.1 copy.28
  60.9 0.0 copy-done.1
  60.9 0.0 copy-start.4
  61.0 0.6 fusion.2
  61.6 0.0 copy-done.2
  61.6 12.3 %fusion = f32[8,512]{1,0:T(8,128)S(1)} fusion(f32[24,512]{1,0:T(8,128)S(1)} %fusion.2), kind=kCustom, calls=%all-reduce-scatter | all-reduce-scatter fusion | flops 16385 | bytes 66048
  73.9 1.7 %collective-permute-start = (f32[6,512]{1,0:T(8,128)S(1)}, f32[6,512]{1,0:T(8,128)S(1)}, u32[]{:S(2)}, u32[]{:S(2)}) collective-permute-start(f32[6,512]{1,0:T(8,128)S(1)} %slice), channel_id=1, source_target_pairs={{0,4},{4,8},{8,12},{1,5},{5,9},{9,13},{2,6},{6,10},{10,14},{3,7},{... | collective-permute-start | bytes 36872
  75.6 0.0 copy-done.4
  75.6 0.6 dynamic-slice.4
  76.8 0.2 collective-permute-done
  77.0 0.1 concatenate
  77.1 0.6 constant_dynamic-slice_fusion
  (4 shorter events, 0.0 us)
Async XLA Ops:
  7.2 44.0 %copy-start = (bf16[256,512]{1,0:T(8,128)(2,1)S(1)}, bf16[256,512]{1,0:T(8,128)(2,1)}, u32[]{:S(2)}) copy-start(bf16[256,512]{1,0:T(8,128)(2,1)} %param.10) | copy-start | bytes 786436
  7.2 42.2 %all-gather.4.cloned.1.call-start = ((), (), s32[]{:S(2)}) async-start(), calls=%async_computation | async-start | bytes 1966080 | tf_op jit(solution)/shard_map/all_gather | solution.py:33
  51.8 7.5 %copy-start.3 = (f32[256,4]{0,1:T(4,128)S(1)}, f32[256,4]{0,1:T(4,128)}, u32[]{:S(2)}) copy-start(f32[256,4]{0,1:T(4,128)} %param.15) | copy-start | bytes 12292
  51.9 9.0 %copy-start.1 = (bf16[24,64,512]{2,1,0:T(8,128)(2,1)S(1)}, bf16[24,64,512]{2,1,0:T(8,128)(2,1)}, u32[]{:S(2)}) copy-start(bf16[24,64,512]{2,1,0:T(8,128)(2,1)} %all-gather.4.cloned.1.call-done) | copy-start | bytes 4718596
  59.2 2.4 %copy-start.2 = (f32[256,4]{0,1:T(4,128)}, f32[256,4]{0,1:T(4,128)S(1)}, u32[]{:S(2)}) copy-start(f32[256,4]{0,1:T(4,128)S(1)} %sub.3) | copy-start | bytes 12292
  60.9 14.6 %copy-start.4 = (u32[32]{0:T(128)S(1)}, u32[32]{0:T(128)}, u32[]{:S(2)}) copy-start(u32[32]{0:T(128)} %constant.19) | copy-start | bytes 388
  73.9 3.1 %collective-permute-start = (f32[6,512]{1,0:T(8,128)S(1)}, f32[6,512]{1,0:T(8,128)S(1)}, u32[]{:S(2)}, u32[]{:S(2)}) collective-permute-start(f32[6,512]{1,0:T(8,128)S(1)} %slice), channel_id=1, source_target_pairs={{0,4},{4,8},{8,12},{1,5},{5,9},{9,13},{2,6},{6,10},{10,14},{3,7},{... | collective-permute-start | bytes 36872
Sparse Core Ops, SparseCore 0:
  9.6 39.7 all-gather.3
